TPU v7x, 256 devices: a whole 4x4x8 slice. The times are simulated.
256 devices in a mesh: dp: 8 (over x, z_hi), tensor: 32 (over y, z_lo, core).
Axes of the slice: x: 4, y: 4, z: 8 (z_hi: 2, z_lo: 4; z = z_hi * 4 + z_lo), core: 2. Of those that a mesh axis runs over, the one named last changes fastest.
Arguments:
- tokens: bfloat16 [8, 4096, 1280], P('dp', 'tensor'), may hold values from -6 to 6
- segment_ids: int32 [8, 4096], P('dp', 'tensor'), may hold values from 0 to 3, never falling along the last dimension, each value on 1 to 2048 neighbouring positions
- pack_of_group: int32 [32], replicated, may hold values from 0 to 31, each once
- w_qkv: bfloat16 [1280, 1920], replicated, may hold values from -0.11320094 to 0.11320094
- qk_gain: float32 [640], replicated, may hold values from 0.5 to 7
- w_out: bfloat16 [640, 1280], replicated, may hold values from -0.25 to 0.25
- alpha_attn: float32 [1280], replicated, may hold values from 0.05 to 0.6
- w_up: bfloat16 [1280, 5120], P(None, 'dp'), may hold values from -0.15625 to 0.15625
- w_gate: bfloat16 [1280, 5120], P(None, 'dp'), may hold values from -0.15625 to 0.15625
- up_gain: float32 [5120], P('dp'), may hold values from 0.5 to 2
- gate_gain: float32 [5120], P('dp'), may hold values from 0.5 to 2
- w_down: bfloat16 [5120, 1280], P('dp'), may hold values from -0.078125 to 0.078125
- alpha_mlp: float32 [1280], replicated, may hold values from 0.05 to 0.6
- w_vocab: bfloat16 [1280, 32000], P(None, ('dp', 'tensor')), may hold values from -0.15625 to 0.15625
- logit_gain: bfloat16 [32000], P(('dp', 'tensor')), may hold values from 1 to 10
Outputs:
- result_rows: bfloat16 [8, 4096, 1280], P('dp', 'tensor')
- request_norm: float32 [32], replicated
- max_logit: float32 [32], replicated
Inputs may be any that keep to these rules, and one draw needn't show every extreme that they name: `segment_ids`: within a pack the request numbers never fall, every request 0 to 3 has one or more tokens, and one request has exactly 2048 tokens.
All inputs are finite; a program needn't handle non-finite values.
Results may differ from a plain program's by a relative error of at most 0.013.
Values may be sent and summed in bfloat16 or wider, within the bound.
No kernel may reach another device: no remote copies, remote signals or barrier semaphores. Data moves between devices by JAX's collectives and lax.ppermute only.
A program may use at most 128 MiB of HBM per device.

v0:
```python
import math
import jax
import jax.numpy as jnp
from jax import lax
from jax.sharding import PartitionSpec as P

HEADS = 10
HD = 64
REQS = 4
EPSILON = 1e-06
NEGATIVE = -1e30


def normalize(values):
    return values * lax.rsqrt(jnp.mean(values * values, axis=-1, keepdims=True) + EPSILON)


def head_norm(values, qk_gain):
    reshaped = values.reshape(values.shape[0], HEADS, HD)
    return (normalize(reshaped) * qk_gain.reshape(HEADS, HD)).astype(jnp.bfloat16)


def local(
    tokens,
    segment_ids,
    pack_of_group,
    w_qkv,
    qk_gain,
    w_out,
    alpha_attn,
    w_up,
    w_gate,
    up_gain,
    gate_gain,
    w_down,
    alpha_mlp,
    w_vocab,
    logit_gain,
):
    row_count = tokens.shape[1]
    head_width = HEADS * HD
    segments = segment_ids[0]
    tensor_index = lax.axis_index("tensor")
    positions = tensor_index * row_count + jnp.arange(row_count, dtype=jnp.int32)
    request_numbers = jnp.arange(REQS, dtype=jnp.int32)
    start_rows = normalize(tokens[0].astype(jnp.float32)).astype(jnp.bfloat16)
    projected = jnp.dot(start_rows, w_qkv, preferred_element_type=jnp.float32)
    queries = head_norm(projected[:, :head_width], qk_gain)
    key_rows = head_norm(projected[:, head_width : 2 * head_width], qk_gain).reshape(
        row_count, head_width
    )
    value_rows = projected[:, 2 * head_width :].astype(jnp.bfloat16)
    score_scale = 1.0 / math.sqrt(HD)
    offset = jnp.int32(0)
    state_now = (
        jnp.full((HEADS, row_count), NEGATIVE, jnp.float32),
        jnp.zeros((HEADS, row_count), jnp.float32),
        jnp.zeros((HEADS, row_count, HD), jnp.float32),
    )
    key_all = lax.all_gather(key_rows, "tensor", axis=0, tiled=True)
    value_all = lax.all_gather(value_rows, "tensor", axis=0, tiled=True)
    seg_all = lax.all_gather(segments, "tensor", axis=0, tiled=True)
    tally = jnp.sum((seg_all[:, None] == request_numbers[None, :]).astype(jnp.int32), axis=0)
    total_keys = key_all.shape[0]
    step_size = math.gcd(total_keys, 512)
    for begin in range(0, total_keys, step_size):
        key_part = key_all[begin : begin + step_size]
        value_part = value_all[begin : begin + step_size]
        seg_part = seg_all[begin : begin + step_size]
        key_pos = offset + begin + jnp.arange(step_size, dtype=jnp.int32)
        update_running_max, update_weight_sum, update_weighted = state_now
        key_count = key_part.shape[0]
        key_heads = key_part.reshape(key_count, HEADS, HD)
        value_heads = value_part.reshape(key_count, HEADS, HD)
        scores = (
            jnp.einsum("qhd,khd->hqk", queries, key_heads, preferred_element_type=jnp.float32)
            * score_scale
        )
        allowed = (seg_part[None, :] == segments[:, None]) & (
            key_pos[None, :] <= positions[:, None]
        )
        new_max = jnp.maximum(
            update_running_max, jnp.max(jnp.where(allowed[None], scores, NEGATIVE), axis=2)
        )
        weights = jnp.where(allowed[None], jnp.exp(scores - new_max[:, :, None]), 0.0)
        factor = jnp.exp(update_running_max - new_max)
        update_weight_sum = update_weight_sum * factor + jnp.sum(weights, axis=2)
        update_weighted = update_weighted * factor[:, :, None] + jnp.einsum(
            "hqk,khd->hqd",
            weights.astype(jnp.bfloat16),
            value_heads,
            preferred_element_type=jnp.float32,
        )
        state_now = (new_max, update_weight_sum, update_weighted)
    folded, tally = (state_now, tally)
    running_max, weight_sum, weighted = folded
    attended = (
        (weighted / weight_sum[:, :, None])
        .transpose(1, 0, 2)
        .reshape(row_count, head_width)
        .astype(jnp.bfloat16)
    )
    attn_rows = normalize(jnp.dot(attended, w_out, preferred_element_type=jnp.float32))
    residual_in = start_rows.astype(jnp.float32)
    mid_rows = normalize(residual_in + alpha_attn * (attn_rows - residual_in)).astype(jnp.bfloat16)
    received = lax.all_gather(mid_rows, "dp", axis=0, tiled=True)
    up_proj = jnp.dot(received, w_up, preferred_element_type=jnp.float32) * up_gain
    gate_proj = jnp.dot(received, w_gate, preferred_element_type=jnp.float32) * gate_gain
    hidden = (up_proj * jax.nn.silu(gate_proj)).astype(jnp.bfloat16)
    mixed_sum = lax.psum_scatter(
        jnp.dot(hidden, w_down, preferred_element_type=jnp.float32).astype(jnp.bfloat16),
        "dp",
        scatter_dimension=0,
        tiled=True,
    ).astype(jnp.float32)
    mlp_rows = normalize(mixed_sum)
    residual_mid = mid_rows.astype(jnp.float32)
    result_rows = normalize(residual_mid + alpha_mlp * (mlp_rows - residual_mid)).astype(
        jnp.bfloat16
    )
    request_ends = jnp.cumsum(tally) - 1
    same_request = segments[:, None] == request_numbers[None, :]
    row_end = jnp.sum(jnp.where(same_request, request_ends[None, :], 0), axis=1)
    is_last = positions == row_end
    member = same_request.astype(jnp.float32)
    chosen = member * is_last[:, None].astype(jnp.float32)
    result_f32 = result_rows.astype(jnp.float32)
    row_sums = jnp.dot(member.T, result_f32, precision=lax.Precision.HIGHEST)
    last_rows = jnp.dot(chosen.T, result_f32, precision=lax.Precision.HIGHEST)
    counts = jnp.sum(member, axis=0)
    row_sums, last_rows, counts = (
        lax.psum(row_sums.astype(jnp.bfloat16), "tensor").astype(jnp.float32),
        lax.psum(last_rows.astype(jnp.bfloat16), "tensor").astype(jnp.float32),
        lax.psum(counts.astype(jnp.bfloat16), "tensor").astype(jnp.float32),
    )
    request_mean = row_sums / counts[:, None]
    group_norm = jnp.sqrt(jnp.mean(request_mean * request_mean, axis=1))
    slot_count = lax.axis_size("dp") * REQS
    every_last, every_norm = (
        lax.all_gather(last_rows, "dp", axis=0, tiled=True),
        lax.all_gather(group_norm, "dp", axis=0, tiled=True),
    )
    logits = jnp.dot(
        every_last.astype(jnp.bfloat16), w_vocab, preferred_element_type=jnp.float32
    ) * logit_gain.astype(jnp.float32)
    every_max = lax.pmax(jnp.max(logits, axis=1), ("dp", "tensor"))
    placement = (pack_of_group[:, None] == jnp.arange(slot_count, dtype=jnp.int32)[None, :]).astype(
        jnp.float32
    )
    request_norm = jnp.dot(every_norm, placement, precision=lax.Precision.HIGHEST)
    max_logit = jnp.dot(every_max, placement, precision=lax.Precision.HIGHEST)
    return (result_rows[None], request_norm, max_logit)


def solution(mesh):
    return jax.shard_map(
        local,
        mesh=mesh,
        in_specs=(
            P("dp", "tensor", None),
            P("dp", "tensor"),
            P(),
            P(),
            P(),
            P(),
            P(),
            P(None, "dp"),
            P(None, "dp"),
            P("dp"),
            P("dp"),
            P("dp", None),
            P(),
            P(None, ("dp", "tensor")),
            P(("dp", "tensor")),
        ),
        out_specs=(P("dp", "tensor", None), P(), P()),
        check_vma=False,
    )
```

profile of v0, /device:TPU:1, one launch (start us, length us, event | category | flops | bytes accessed | tf_op | source)
XLA Modules:
  0.0 689.7 jit_solution(16697699601182889394)
XLA Ops:
  7.2 1.2 fusion.143
  8.5 3.4 fusion.186
  11.9 0.7 slice.147
  13.1 0.7 multiply_convert_fusion.3
  14.2 46.0 %all-gather = s32[1,4096]{1,0:T(1,128)S(1)} all-gather(s32[1,128]{1,0:T(1,128)S(1)} %copy-done.26), channel_id=2, replica_groups=mesh['dp'=8,'tensor'=32] {'tensor'}, dimensions={1}, use_global_device_ids=true | all-gather | bytes 16896 | tf_op jit(solution)/shard_map/all_gather | solution.py:62
  60.5 1.2 fusion.145
  61.7 19.2 %all-gather.8.cloned.1.call-done = bf16[4096,640]{1,0:T(8,128)(2,1)} async-done(((bf16[128,640]{1,0:T(8,128)(2,1)}), bf16[4096,640]{1,0:T(8,128)(2,1)}) %all-gather.8.cloned.1.call-update) | async-done | bytes 5242896 | tf_op jit(solution)/shard_map/all_gather | solution.py:61
  80.8 4.5 fusion.191
  85.3 2.2 copy.88
  87.5 58.2 %all-gather.6.cloned.1.call-done = bf16[4096,640]{1,0:T(8,128)(2,1)} async-done(((bf16[128,640]{1,0:T(8,128)(2,1)}), bf16[4096,640]{1,0:T(8,128)(2,1)}) %all-gather.6.cloned.1.call-update) | async-done | bytes 5242896 | tf_op jit(solution)/shard_map/all_gather | solution.py:60
  145.7 4.9 fusion.192
  150.6 2.2 copy.77
  152.8 2.2 copy.91
  154.9 2.2 copy.89
  157.1 2.2 copy.87
  159.3 2.2 copy.85
  161.5 2.2 copy.83
  163.7 2.2 copy.81
  165.9 2.2 copy.79
  168.1 2.2 copy.92
  170.3 2.2 copy.90
  172.4 2.2 copy.86
  174.6 2.2 copy.84
  176.8 2.2 copy.82
  179.0 1.1 copy.80
  180.1 1.1 copy.78
  181.2 1.8 select_reduce_fusion.6
  183.0 0.7 select_reduce_fusion.5
  184.1 0.7 select_reduce_fusion.4
  184.8 0.7 select_reduce_fusion.3
  185.8 0.7 select_reduce_fusion.2
  186.6 0.7 select_reduce_fusion.1
  187.6 0.7 select_reduce_fusion
  188.4 0.7 select_reduce_fusion.7
  189.4 0.7 fusion.97
  190.2 1.8 fusion.4
  192.0 0.7 fusion.100
  193.1 0.7 fusion.124
  193.9 1.6 fusion.12
  195.5 0.7 fusion.127
  196.6 0.7 fusion.94
  197.3 1.6 fusion
  199.0 0.7 fusion.103
  199.7 1.6 fusion.8
  201.4 0.8 fusion.130
  202.5 0.8 fusion.137
  203.3 0.6 copy-done.11
  203.9 0.5 multiply_reduce_fusion.2
  204.8 1.0 multiply_convert_fusion.2
  206.1 81.0 %all-gather.10.cloned.1.call-done = bf16[1024,1280]{1,0:T(8,128)(2,1)} async-done(((bf16[128,1280]{1,0:T(8,128)(2,1)}), bf16[1024,1280]{1,0:T(8,128)(2,1)}) %all-gather.10.cloned.1.call-update) | async-done | bytes 2621456 | tf_op jit(solution)/shard_map/all_gather | solution.py:106
  287.2 5.9 fusion.194
  293.1 8.4 %convolution_convert_fusion = bf16[1024,1280]{1,0:T(8,128)(2,1)} fusion(bf16[640,1280]{1,0:T(8,128)(2,1)S(1)} %copy-done, f32[1024,640]{1,0:T(8,128)} %fusion.194, bf16[1024,1280]{1,0:T(8,128)(2,1)} %all-gather.10.cloned.1.call-done, bf16[1280,640]{1,0:T(8,128)(2,1)S(1)} %copy-done.27, f32[640]{0:T(1024)S(1)} %copy-done.28, f32[640]{0:T(1024)S(1)} %copy-done.29), kind=kOutput, calls=%fused_computation | convolution fusion | flops 3361996800 | bytes 11146240 | tf_op jit(solution)/shard_map/dot_general | solution.py:111
  301.6 0.6 copy-done.30
  302.2 0.6 dynamic-slice
  304.0 94.9 %reduce-scatter.2.cloned.1.call-done = bf16[128,1280]{1,0:T(8,128)(2,1)} async-done(((bf16[1024,1280]{1,0:T(8,128)(2,1)}), bf16[128,1280]{1,0:T(8,128)(2,1)}) %reduce-scatter.2.cloned.1.call-update) | async-done | bytes 327696 | tf_op jit(solution)/shard_map/reduce_scatter | solution.py:110
  398.9 1.1 fusion.142
  400.1 1.3 multiply_reduce_fusion
  401.4 1.4 multiply_convert_fusion.1
  403.2 130.5 %all-reduce.1 = (bf16[4,1280]{1,0:T(4,128)(2,1)S(1)}, bf16[4]{0:T(256)(128)(2,1)S(1)}, bf16[4,1280]{1,0:T(4,128)(2,1)S(1)}) all-reduce(bf16[4,1280]{1,0:T(4,128)(2,1)S(1)} %convolution_convert_fusion.2, bf16[4]{0:T(256)(128)(2,1)S(1)} %convert_reduce_fusion.1, ...), channel_id=1, replica_groups=mesh['dp'=8,'tensor'=32] {'tensor'}, use_global_device_ids=true, to_apply=%region_24.25 | all-reduce | flops 10244 | bytes 40976 | tf_op jit(solution)/shard_map/psum | solution.py:132
  533.7 37.8 %all-gather.1 = bf16[8,4,1280]{2,1,0:T(4,128)(2,1)S(1)} all-gather(bf16[1,4,1280]{2,1,0:T(4,128)(2,1)S(1)} %bitcast.282), channel_id=1, replica_groups=mesh['dp'=8,'tensor'=32] {'dp'}, dimensions={0}, use_global_device_ids=true | all-gather | bytes 92160 | tf_op jit(solution)/shard_map/all_gather | solution.py:140
  572.1 23.2 %all-reduce = f32[32]{0:T(128)S(1)} all-reduce(f32[32]{0:T(128)S(1)} %sqrt_dynamic-update-slice_fusion), channel_id=1, replica_groups=mesh['dp'=8,'tensor'=32] {'dp'}, use_global_device_ids=true, to_apply=%add | all-reduce | flops 32 | bytes 256
  595.3 86.5 %pmax.7 = f32[32]{0:T(128)S(1)} all-reduce(f32[32]{0:T(128)S(1)} %fusion.133), channel_id=1, replica_groups=mesh['dp'=8,'tensor'=32] {'dp','tensor'}, use_global_device_ids=true, to_apply=%region_33.34 | all-reduce | flops 32 | bytes 256 | tf_op jit(solution)/shard_map/pmax | solution.py:146
  681.8 0.7 convolution_bitcast_fusion.1
  682.5 0.7 convolution_bitcast_fusion
  (116 shorter events, 6.0 us)
Async XLA Ops:
  7.2 285.9 %copy-start = (bf16[640,1280]{1,0:T(8,128)(2,1)S(1)}, bf16[640,1280]{1,0:T(8,128)(2,1)}, u32[]{:S(2)}) copy-start(bf16[640,1280]{1,0:T(8,128)(2,1)} %param.26) | copy-start | bytes 4915204
  7.2 73.7 %all-gather.8.cloned.1.call-start = ((), (), s32[]{:S(2)}) async-start(), calls=%async_computation.2 | async-start | bytes 5406720 | tf_op jit(solution)/shard_map/all_gather | solution.py:61
  11.9 1.2 copy-start.25
  12.6 1.6 copy-start.26
  12.6 133.1 %all-gather.6.cloned.1.call-start = ((), (), s32[]{:S(2)}) async-start(), calls=%async_computation.1 | async-start | bytes 5406720 | tf_op jit(solution)/shard_map/all_gather | solution.py:60
  13.9 273.3 %all-gather.10.cloned.1.call-start = ((), (), s32[]{:S(2)}) async-start(), calls=%async_computation.3 | async-start | bytes 2949120 | tf_op jit(solution)/shard_map/all_gather | solution.py:106
  180.1 2.9 copy-start.10
  181.2 1.8 copy-start.21
  183.0 1.1 copy-start.9
  183.0 1.1 copy-start.20
  183.7 1.1 copy-start.8
  184.7 1.1 copy-start.7
  185.5 1.1 copy-start.6
  186.5 1.1 copy-start.5
  187.3 1.1 copy-start.4
  188.3 1.1 copy-start.19
  190.2 1.8 copy-start.18
  192.0 1.1 copy-start.17
  193.8 1.6 copy-start.15
  195.5 1.1 copy-start.16
  197.3 1.6 copy-start.14
  199.7 1.7 copy-start.13
  201.4 1.1 copy-start.12
  202.5 1.4 copy-start.11
  202.5 2.0 copy-start.23
  203.3 1.2 copy-start.1
  205.8 87.3 %copy-start.27 = (bf16[1280,640]{1,0:T(8,128)(2,1)S(1)}, bf16[1280,640]{1,0:T(8,128)(2,1)}, u32[]{:S(2)}) copy-start(bf16[1280,640]{1,0:T(8,128)(2,1)} %param.23) | copy-start | bytes 4915204
  205.8 87.2 %copy-start.28 = (f32[640]{0:T(1024)S(1)}, f32[640]{0:T(1024)}, u32[]{:S(2)}) copy-start(f32[640]{0:T(1024)} %param.25) | copy-start | bytes 7684
  205.8 87.2 %copy-start.29 = (f32[640]{0:T(1024)S(1)}, f32[640]{0:T(1024)}, u32[]{:S(2)}) copy-start(f32[640]{0:T(1024)} %param.24) | copy-start | bytes 7684
  205.9 193.1 %reduce-scatter.2.cloned.1.call-start = ((), (), s32[]{:S(2)}) async-start(), calls=%async_computation.4 | async-start | bytes 2949120 | tf_op jit(solution)/shard_map/reduce_scatter | solution.py:110
  301.5 0.7 copy-start.30
  301.5 0.7 copy-start.32
  301.5 98.5 %copy-start.2 = (bf16[128,1280]{1,0:T(8,128)(2,1)S(1)}, bf16[128,1280]{1,0:T(8,128)(2,1)}, u32[]{:S(2)}) copy-start(bf16[128,1280]{1,0:T(8,128)(2,1)} %multiply_convert_fusion.2) | copy-start | bytes 983044
  301.5 98.5 %copy-start.24 = (f32[1280]{0:T(1024)S(1)}, f32[1280]{0:T(1024)}, u32[]{:S(2)}) copy-start(f32[1280]{0:T(1024)} %param.27) | copy-start | bytes 15364
  301.5 270.3 %copy-start.22 = (bf16[1280,125]{1,0:T(8,128)(2,1)S(1)}, bf16[1280,125]{1,0:T(8,128)(2,1)}, u32[]{:S(2)}) copy-start(bf16[1280,125]{1,0:T(8,128)(2,1)} %param.28) | copy-start | bytes 960004
  301.5 380.2 %copy-start.31 = (s32[32]{0:T(128)S(1)}, s32[32]{0:T(128)}, u32[]{:S(2)}) copy-start(s32[32]{0:T(128)} %param.17) | copy-start | bytes 388
  402.8 280.4 %copy-start.3 = (bf16[128,1280]{1,0:T(8,128)(2,1)}, bf16[128,1280]{1,0:T(8,128)(2,1)S(1)}, u32[]{:S(2)}) copy-start(bf16[128,1280]{1,0:T(8,128)(2,1)S(1)} %multiply_convert_fusion.1) | copy-start | bytes 983044
Sparse Core Ops, SparseCore 0:
  12.7 68.0 all-gather.7
  82.7 62.9 all-gather.5
  205.9 81.1 all-gather.9
  301.7 97.1 reduce-scatter.1
where the time goes:
time: 691 us; the launch traced here: 690 us
  blocking collectives  324 us (47%)
  waiting for transfers between devices  253 us (37%)
  local copies, waits for them, and re-layouts  47.8 us (7%)
  matrix products  33 us (5%)
  other arithmetic  16.1 us (2%)
  between operations  15 us (2%)
    psum x1, blocking collectives, local(): lax.psum(row_sums.astype(jnp.bfloat16), 'tensor').astype(jnp.float32)  131 us
    reduce_scatter x1, waiting for transfers between devices, local(): lax.psum_scatter(jnp.dot(hidden, w_down, preferred_element_type=jnp.float...  94.9 us
    pmax x1, blocking collectives, local(): every_max = lax.pmax(jnp.max(logits, axis=1), ('dp', 'tensor'))  86.5 us
    all_gather x1, waiting for transfers between devices, local(): received = lax.all_gather(mid_rows, 'dp', axis=0, tiled=True)  81 us
    all_gather x1, waiting for transfers between devices, local(): key_all = lax.all_gather(key_rows, 'tensor', axis=0, tiled=True)  58.2 us
    all_gather x1, blocking collectives, local(): seg_all = lax.all_gather(segments, 'tensor', axis=0, tiled=True)  46 us
    all_gather x1, blocking collectives, local(): lax.all_gather(last_rows, 'dp', axis=0, tiled=True)  37.8 us
    unnamed x1, blocking collectives  23.2 us
  transfers between devices with their start and end apart: 4, of which 4 were waited for; matrix products, arithmetic and copies ran while one was open for 2% of the time, Pallas kernels for 0%

commit v1 on v0

--- a/solution.py
+++ b/solution.py
@@ -129,7 +129,9 @@
     last_rows = jnp.dot(chosen.T, result_f32, precision=lax.Precision.HIGHEST)
     counts = jnp.sum(member, axis=0)
     row_sums, last_rows, counts = (
-        lax.psum(row_sums.astype(jnp.bfloat16), "tensor").astype(jnp.float32),
+        jnp.sum(lax.all_gather(row_sums.astype(jnp.bfloat16), "tensor"), axis=0).astype(
+            jnp.float32
+        ),
         lax.psum(last_rows.astype(jnp.bfloat16), "tensor").astype(jnp.float32),
         lax.psum(counts.astype(jnp.bfloat16), "tensor").astype(jnp.float32),
     )

time: 691 us -> 732 us (1.059)
  blocking collectives: 324 us -> 364 us
    all_gather x0 -> x1, blocking collectives: none -> 43.3 us  [local(): lax.all_gather(row_sums.astype(jnp.bfloat16), 'tensor')]
  transfers between devices with their start and end apart: 4 -> 4, of which waited for: 4 -> 4; matrix products, arithmetic and copies ran while one was open for 2% -> 1% of each run, Pallas kernels for 0% -> 0%
where the time goes in v1:
time: 732 us; the launch traced here: 730 us
  blocking collectives  364 us (50%)
  waiting for transfers between devices  253 us (35%)
  local copies, waits for them, and re-layouts  47.8 us (7%)
  matrix products  33 us (5%)
  other arithmetic  16.3 us (2%)
  between operations  15 us (2%)
    psum x1, blocking collectives, local(): lax.psum(counts.astype(jnp.bfloat16), 'tensor').astype(jnp.float32)  131 us
    reduce_scatter x1, waiting for transfers between devices, local(): lax.psum_scatter(jnp.dot(hidden, w_down, preferred_element_type=jnp.float...  94.9 us
    pmax x1, blocking collectives, local(): every_max = lax.pmax(jnp.max(logits, axis=1), ('dp', 'tensor'))  82.9 us
    all_gather x1, waiting for transfers between devices, local(): received = lax.all_gather(mid_rows, 'dp', axis=0, tiled=True)  81 us
    all_gather x1, waiting for transfers between devices, local(): key_all = lax.all_gather(key_rows, 'tensor', axis=0, tiled=True)  58.2 us
    all_gather x1, blocking collectives, local(): seg_all = lax.all_gather(segments, 'tensor', axis=0, tiled=True)  46 us
    all_gather x1, blocking collectives, local(): lax.all_gather(row_sums.astype(jnp.bfloat16), 'tensor')  43.3 us
    all_gather x1, blocking collectives, local(): lax.all_gather(last_rows, 'dp', axis=0, tiled=True)  37.7 us
  transfers between devices with their start and end apart: 4, of which 4 were waited for; matrix products, arithmetic and copies ran while one was open for 1% of the time, Pallas kernels for 0%

profile of v1, /device:TPU:1, one launch (start us, length us, event | category | flops | bytes accessed | tf_op | source)
XLA Modules:
  0.0 729.9 jit_solution(922582005389861080)
XLA Ops:
  7.2 1.2 fusion.144
  8.5 3.4 fusion.187
  11.9 0.7 slice.147
  13.1 0.7 multiply_convert_fusion.3
  14.2 46.0 %all-gather = s32[1,4096]{1,0:T(1,128)S(1)} all-gather(s32[1,128]{1,0:T(1,128)S(1)} %copy-done.26), channel_id=2, replica_groups=mesh['dp'=8,'tensor'=32] {'tensor'}, dimensions={1}, use_global_device_ids=true | all-gather | bytes 16896 | tf_op jit(solution)/shard_map/all_gather | solution.py:62
  60.5 1.2 fusion.146
  61.7 19.2 %all-gather.10.cloned.1.call-done = bf16[4096,640]{1,0:T(8,128)(2,1)} async-done(((bf16[128,640]{1,0:T(8,128)(2,1)}), bf16[4096,640]{1,0:T(8,128)(2,1)}) %all-gather.10.cloned.1.call-update) | async-done | bytes 5242896 | tf_op jit(solution)/shard_map/all_gather | solution.py:61
  80.8 4.5 fusion.192
  85.3 2.2 copy.88
  87.5 58.2 %all-gather.8.cloned.1.call-done = bf16[4096,640]{1,0:T(8,128)(2,1)} async-done(((bf16[128,640]{1,0:T(8,128)(2,1)}), bf16[4096,640]{1,0:T(8,128)(2,1)}) %all-gather.8.cloned.1.call-update) | async-done | bytes 5242896 | tf_op jit(solution)/shard_map/all_gather | solution.py:60
  145.7 4.9 fusion.193
  150.6 2.2 copy.77
  152.8 2.2 copy.91
  154.9 2.2 copy.89
  157.1 2.2 copy.87
  159.3 2.2 copy.85
  161.5 2.2 copy.83
  163.7 2.2 copy.81
  165.9 2.2 copy.79
  168.1 2.2 copy.92
  170.3 2.2 copy.90
  172.4 2.2 copy.86
  174.6 2.2 copy.84
  176.8 2.2 copy.82
  179.0 1.1 copy.80
  180.1 1.1 copy.78
  181.2 1.8 select_reduce_fusion.6
  183.0 0.7 select_reduce_fusion.5
  184.1 0.7 select_reduce_fusion.4
  184.8 0.7 select_reduce_fusion.3
  185.8 0.7 select_reduce_fusion.2
  186.6 0.7 select_reduce_fusion.1
  187.6 0.7 select_reduce_fusion
  188.4 0.7 select_reduce_fusion.7
  189.4 0.7 fusion.98
  190.2 1.8 fusion.5
  192.0 0.7 fusion.101
  193.1 0.7 fusion.125
  193.9 1.6 fusion.13
  195.5 0.7 fusion.128
  196.6 0.7 fusion.95
  197.3 1.6 fusion.1
  199.0 0.7 fusion.104
  199.7 1.6 fusion.9
  201.4 0.8 fusion.131
  202.5 0.8 fusion.138
  203.3 0.6 copy-done.11
  204.8 1.0 multiply_convert_fusion.2
  206.1 81.0 %all-gather.12.cloned.1.call-done = bf16[1024,1280]{1,0:T(8,128)(2,1)} async-done(((bf16[128,1280]{1,0:T(8,128)(2,1)}), bf16[1024,1280]{1,0:T(8,128)(2,1)}) %all-gather.12.cloned.1.call-update) | async-done | bytes 2621456 | tf_op jit(solution)/shard_map/all_gather | solution.py:106
  287.2 5.9 fusion.195
  293.1 8.4 %convolution_convert_fusion = bf16[1024,1280]{1,0:T(8,128)(2,1)} fusion(bf16[640,1280]{1,0:T(8,128)(2,1)S(1)} %copy-done, f32[1024,640]{1,0:T(8,128)} %fusion.195, bf16[1024,1280]{1,0:T(8,128)(2,1)} %all-gather.12.cloned.1.call-done, bf16[1280,640]{1,0:T(8,128)(2,1)S(1)} %copy-done.27, f32[640]{0:T(1024)S(1)} %copy-done.28, f32[640]{0:T(1024)S(1)} %copy-done.29), kind=kOutput, calls=%fused_computation | convolution fusion | flops 3361996800 | bytes 11146240 | tf_op jit(solution)/shard_map/dot_general | solution.py:111
  301.6 0.6 copy-done.30
  302.2 0.6 dynamic-slice
  304.0 94.9 %reduce-scatter.2.cloned.1.call-done = bf16[128,1280]{1,0:T(8,128)(2,1)} async-done(((bf16[1024,1280]{1,0:T(8,128)(2,1)}), bf16[128,1280]{1,0:T(8,128)(2,1)}) %reduce-scatter.2.cloned.1.call-update) | async-done | bytes 327696 | tf_op jit(solution)/shard_map/reduce_scatter | solution.py:110
  398.9 1.1 fusion.143
  400.1 1.3 multiply_reduce_fusion
  401.4 1.4 multiply_convert_fusion.1
  403.2 130.6 %all-reduce.1 = (bf16[4]{0:T(256)(128)(2,1)S(1)}, bf16[4,1280]{1,0:T(4,128)(2,1)S(1)}) all-reduce(bf16[4]{0:T(256)(128)(2,1)S(1)} %convert_reduce_fusion.1, bf16[4,1280]{1,0:T(4,128)(2,1)S(1)} %convolution_convert_fusion.1), channel_id=1, replica_groups=mesh['dp'=8,'tensor'=32] {'tensor'}, use_global_device_ids=true, to_apply=%region_26.27 | all-reduce | flops 5124 | bytes 20496 | tf_op jit(solution)/shard_map/psum | solution.py:136
  533.7 37.7 %all-gather.3 = bf16[8,4,1280]{2,1,0:T(4,128)(2,1)S(1)} all-gather(bf16[1,4,1280]{2,1,0:T(4,128)(2,1)S(1)} %bitcast.284), channel_id=1, replica_groups=mesh['dp'=8,'tensor'=32] {'dp'}, dimensions={0}, use_global_device_ids=true | all-gather | bytes 92160 | tf_op jit(solution)/shard_map/all_gather | solution.py:142
  571.8 82.9 %pmax.7 = f32[32]{0:T(128)S(1)} all-reduce(f32[32]{0:T(128)S(1)} %fusion.134), channel_id=1, replica_groups=mesh['dp'=8,'tensor'=32] {'dp','tensor'}, use_global_device_ids=true, to_apply=%region_33.34 | all-reduce | flops 32 | bytes 256 | tf_op jit(solution)/shard_map/pmax | solution.py:148
  654.7 43.3 %all-gather.2 = bf16[32,4,1280]{2,1,0:T(4,128)(2,1)S(1)} all-gather(bf16[1,4,1280]{2,1,0:T(4,128)(2,1)S(1)} %fusion), channel_id=3, replica_groups=mesh['dp'=8,'tensor'=32] {'tensor'}, dimensions={0}, use_global_device_ids=true | all-gather | bytes 337920 | tf_op jit(solution)/shard_map/all_gather | solution.py:132
  698.4 23.6 %all-reduce = f32[32]{0:T(128)S(1)} all-reduce(f32[32]{0:T(128)S(1)} %sqrt_dynamic-update-slice_fusion), channel_id=1, replica_groups=mesh['dp'=8,'tensor'=32] {'dp'}, use_global_device_ids=true, to_apply=%add | all-reduce | flops 32 | bytes 256
  722.0 0.7 convolution_bitcast_fusion
  722.7 0.7 convolution_bitcast_fusion.1
  (118 shorter events, 6.6 us)
Async XLA Ops:
  7.2 285.9 %copy-start = (bf16[640,1280]{1,0:T(8,128)(2,1)S(1)}, bf16[640,1280]{1,0:T(8,128)(2,1)}, u32[]{:S(2)}) copy-start(bf16[640,1280]{1,0:T(8,128)(2,1)} %param.26) | copy-start | bytes 4915204
  7.2 73.7 %all-gather.10.cloned.1.call-start = ((), (), s32[]{:S(2)}) async-start(), calls=%async_computation.2 | async-start | bytes 5406720 | tf_op jit(solution)/shard_map/all_gather | solution.py:61
  11.9 1.2 copy-start.25
  12.6 1.6 copy-start.26
  12.6 133.1 %all-gather.8.cloned.1.call-start = ((), (), s32[]{:S(2)}) async-start(), calls=%async_computation.1 | async-start | bytes 5406720 | tf_op jit(solution)/shard_map/all_gather | solution.py:60
  13.9 273.3 %all-gather.12.cloned.1.call-start = ((), (), s32[]{:S(2)}) async-start(), calls=%async_computation.3 | async-start | bytes 2949120 | tf_op jit(solution)/shard_map/all_gather | solution.py:106
  180.1 2.9 copy-start.10
  181.2 1.8 copy-start.21
  183.0 1.1 copy-start.9
  183.0 1.1 copy-start.20
  183.7 1.1 copy-start.8
  184.7 1.1 copy-start.7
  185.5 1.1 copy-start.6
  186.5 1.1 copy-start.5
  187.3 1.1 copy-start.4
  188.3 1.1 copy-start.19
  190.2 1.8 copy-start.18
  192.0 1.1 copy-start.17
  193.8 1.6 copy-start.15
  195.5 1.1 copy-start.16
  197.3 1.6 copy-start.14
  199.7 1.7 copy-start.13
  201.4 1.1 copy-start.12
  202.5 1.4 copy-start.11
  202.5 2.0 copy-start.23
  203.3 1.2 copy-start.1
  205.8 87.3 %copy-start.27 = (bf16[1280,640]{1,0:T(8,128)(2,1)S(1)}, bf16[1280,640]{1,0:T(8,128)(2,1)}, u32[]{:S(2)}) copy-start(bf16[1280,640]{1,0:T(8,128)(2,1)} %param.23) | copy-start | bytes 4915204
  205.8 87.2 %copy-start.28 = (f32[640]{0:T(1024)S(1)}, f32[640]{0:T(1024)}, u32[]{:S(2)}) copy-start(f32[640]{0:T(1024)} %param.25) | copy-start | bytes 7684
  205.8 87.2 %copy-start.29 = (f32[640]{0:T(1024)S(1)}, f32[640]{0:T(1024)}, u32[]{:S(2)}) copy-start(f32[640]{0:T(1024)} %param.24) | copy-start | bytes 7684
  205.9 193.0 %reduce-scatter.2.cloned.1.call-start = ((), (), s32[]{:S(2)}) async-start(), calls=%async_computation.4 | async-start | bytes 2949120 | tf_op jit(solution)/shard_map/reduce_scatter | solution.py:110
  301.5 0.7 copy-start.30
  301.5 0.7 copy-start.32
  301.5 98.5 %copy-start.2 = (bf16[128,1280]{1,0:T(8,128)(2,1)S(1)}, bf16[128,1280]{1,0:T(8,128)(2,1)}, u32[]{:S(2)}) copy-start(bf16[128,1280]{1,0:T(8,128)(2,1)} %multiply_convert_fusion.2) | copy-start | bytes 983044
  301.5 98.5 %copy-start.24 = (f32[1280]{0:T(1024)S(1)}, f32[1280]{0:T(1024)}, u32[]{:S(2)}) copy-start(f32[1280]{0:T(1024)} %param.27) | copy-start | bytes 15364
  301.5 269.9 %copy-start.22 = (bf16[1280,125]{1,0:T(8,128)(2,1)S(1)}, bf16[1280,125]{1,0:T(8,128)(2,1)}, u32[]{:S(2)}) copy-start(bf16[1280,125]{1,0:T(8,128)(2,1)} %param.28) | copy-start | bytes 960004
  301.6 420.4 %copy-start.31 = (s32[32]{0:T(128)S(1)}, s32[32]{0:T(128)}, u32[]{:S(2)}) copy-start(s32[32]{0:T(128)} %param.17) | copy-start | bytes 388
  402.7 320.7 %copy-start.3 = (bf16[128,1280]{1,0:T(8,128)(2,1)}, bf16[128,1280]{1,0:T(8,128)(2,1)S(1)}, u32[]{:S(2)}) copy-start(bf16[128,1280]{1,0:T(8,128)(2,1)S(1)} %multiply_convert_fusion.1) | copy-start | bytes 983044
Sparse Core Ops, SparseCore 0:
  12.7 68.0 all-gather.9
  82.7 62.9 all-gather.7
  205.9 81.1 all-gather.11
  301.7 97.1 reduce-scatter.1
